TPU v7x, 256 devices: a whole 4x4x8 slice. The times are simulated.
256 devices in a mesh: rep: 16 (over z, core), exp: 16 (over y, x).
Axes of the slice: x: 4, y: 4, z: 8, core: 2. Of those that a mesh axis runs over, the one named last changes fastest.
Arguments:
- tokens: bfloat16 [2048, 2048], P('exp'), may hold values from -6 to 6
- expert_ids: int32 [2048, 2], P('exp'), may hold values from 0 to 15, all different within a row; in each aligned block of 128 rows (0 to 127, 128 to 255, ...) at most 32 rows name the same one
- gate_values: float32 [2048, 2], P('exp'), may hold values from 0.2 to 1
- grad_out: bfloat16 [2048, 2048], P('exp'), may hold values from -6 to 6
- w_up: bfloat16 [16, 2048, 8192], P('exp', None, 'rep'), may hold values from -0.125 to 0.125
- w_down: bfloat16 [16, 8192, 2048], P('exp', 'rep'), may hold values from -0.0625 to 0.0625
Outputs:
- mixed: bfloat16 [2048, 2048], P('exp', 'rep')
- grad_tokens: bfloat16 [2048, 2048], P('exp', 'rep')
- grad_w_up: bfloat16 [16, 2048, 8192], P('exp', None, 'rep')
- grad_w_down: bfloat16 [16, 8192, 2048], P('exp', 'rep')
Inputs may be any that keep to these rules, and one draw needn't show every extreme that they name: `expert_ids`: each row names 2 different experts. Within the rows of one index of exp (aligned blocks of 128 rows) no expert is named by more than 32 rows, a bound that some block reaches.
All inputs are finite; a program needn't handle non-finite values.
Results may differ from a plain program's by a relative error of at most 0.022.
Values may be sent and summed in bfloat16 or wider, within the bound.
No kernel may reach another device: no remote copies, remote signals or barrier semaphores. Data moves between devices by JAX's collectives and lax.ppermute only.
A program may use at most 128 MiB of HBM per device.

v0:
```python
import jax
import jax.numpy as jnp
from jax import lax
from jax.sharding import PartitionSpec as P


def plan_slots(routed, experts, capacity):
    flat_ids = routed.reshape(-1)
    onehot = (flat_ids[:, None] == jnp.arange(experts, dtype=jnp.int32)[None, :]).astype(jnp.int32)
    before = jnp.cumsum(onehot, axis=0) - onehot
    position = jnp.sum(before * onehot, axis=1)
    counts = jnp.sum(onehot, axis=0)
    slotting_labels = flat_ids * capacity + position
    placed = (
        slotting_labels[None, :] == jnp.arange(experts * capacity, dtype=jnp.int32)[:, None]
    ).astype(jnp.bfloat16)
    return (placed, counts)


def expert_math(rows_in, rows_grad, live_mask, up_weight, down_weight):
    preact = jnp.dot(rows_in, up_weight, preferred_element_type=jnp.float32)
    sigmoid_val = jax.nn.sigmoid(preact)
    keep = live_mask[:, None]
    hidden_units = jnp.where(keep, preact * sigmoid_val, 0.0).astype(jnp.bfloat16)
    out_part = jnp.dot(hidden_units, down_weight, preferred_element_type=jnp.float32)
    grad_hidden = lax.dot_general(
        rows_grad, down_weight, (((1,), (1,)), ((), ())), preferred_element_type=jnp.float32
    )
    slope = sigmoid_val * (1.0 + preact * (1.0 - sigmoid_val))
    gradient_before_activation = jnp.where(keep, grad_hidden * slope, 0.0).astype(jnp.bfloat16)
    grad_down_e = lax.dot_general(
        hidden_units, rows_grad, (((0,), (0,)), ((), ())), preferred_element_type=jnp.float32
    )
    grad_up_e = lax.dot_general(
        rows_in,
        gradient_before_activation,
        (((0,), (0,)), ((), ())),
        preferred_element_type=jnp.float32,
    )
    dx_part = lax.dot_general(
        gradient_before_activation,
        up_weight,
        (((1,), (1,)), ((), ())),
        preferred_element_type=jnp.float32,
    )
    return (out_part, dx_part, grad_up_e, grad_down_e)


def local(tokens, expert_ids, gate_values, grad_out, w_up, w_down):
    n_rep = lax.axis_size("rep")
    n_exp = lax.axis_size("exp")
    tok_count, width = tokens.shape
    top_k = expert_ids.shape[1]
    pair_count = tok_count * top_k
    capacity = max(2, min(tok_count, 2 * tok_count * top_k // n_exp))
    cols = width // n_rep
    up_weight = w_up[0]
    down_weight = w_down[0]
    grad_rows = (gate_values[:, :, None] * grad_out[:, None, :].astype(jnp.float32)).astype(
        jnp.bfloat16
    )
    grad_rows = grad_rows.reshape(pair_count, width)
    placed, counts = plan_slots(expert_ids, n_exp, capacity)
    summed = placed.reshape(n_exp * capacity, tok_count, top_k).sum(axis=2)
    sent_in = jnp.dot(summed, tokens, preferred_element_type=jnp.float32).astype(jnp.bfloat16)
    sent_grad = jnp.dot(placed, grad_rows, preferred_element_type=jnp.float32).astype(jnp.bfloat16)
    count_parts = jnp.stack([counts // 16, counts % 16], axis=1).astype(jnp.bfloat16)
    got_in, got_grad, got_counts = (
        lax.all_to_all(
            sent_in.reshape(n_exp, capacity, width), "exp", split_axis=0, concat_axis=0, tiled=True
        ),
        lax.all_to_all(
            sent_grad.reshape(n_exp, capacity, width),
            "exp",
            split_axis=0,
            concat_axis=0,
            tiled=True,
        ),
        lax.all_to_all(count_parts, "exp", split_axis=0, concat_axis=0, tiled=True),
    )
    count_values = got_counts[:, 0].astype(jnp.float32) * 16.0 + got_counts[:, 1].astype(
        jnp.float32
    )
    slot_mask = jnp.arange(capacity, dtype=jnp.float32)[None, :] < count_values[:, None]
    rows_in = got_in.reshape(-1, width)
    rows_grad = got_grad.reshape(-1, width)
    live_mask = slot_mask.reshape(-1)
    out_part, dx_part, grad_up_e, grad_down_e = expert_math(
        rows_in, rows_grad, live_mask, up_weight, down_weight
    )
    total_out, total_dx = (
        lax.psum(out_part.astype(jnp.bfloat16), "rep").astype(jnp.float32),
        lax.psum(dx_part.astype(jnp.bfloat16), "rep").astype(jnp.float32),
    )
    col_start = lax.axis_index("rep") * cols
    summed_out = lax.dynamic_slice_in_dim(total_out, col_start, cols, 1)
    summed_dx = lax.dynamic_slice_in_dim(total_dx, col_start, cols, 1)
    back_out, back_dx = (
        lax.all_to_all(
            summed_out.astype(jnp.bfloat16).reshape(n_exp, capacity, cols),
            "exp",
            split_axis=0,
            concat_axis=0,
            tiled=True,
        ),
        lax.all_to_all(
            summed_dx.astype(jnp.bfloat16).reshape(n_exp, capacity, cols),
            "exp",
            split_axis=0,
            concat_axis=0,
            tiled=True,
        ),
    )
    pair_out = jnp.einsum(
        "st,sd->td",
        placed,
        back_out.reshape(n_exp * capacity, cols),
        preferred_element_type=jnp.float32,
    )
    pair_dx = jnp.einsum(
        "st,sd->td",
        placed,
        back_dx.reshape(n_exp * capacity, cols),
        preferred_element_type=jnp.float32,
    )
    mixed = jnp.sum(gate_values[:, :, None] * pair_out.reshape(tok_count, top_k, cols), axis=1)
    grad_tokens = jnp.sum(pair_dx.reshape(tok_count, top_k, cols), axis=1)
    return (
        mixed.astype(jnp.bfloat16),
        grad_tokens.astype(jnp.bfloat16),
        grad_up_e.astype(jnp.bfloat16)[None],
        grad_down_e.astype(jnp.bfloat16)[None],
    )


def solution(mesh):
    return jax.shard_map(
        local,
        mesh=mesh,
        in_specs=(
            P("exp", None),
            P("exp", None),
            P("exp", None),
            P("exp", None),
            P("exp", None, "rep"),
            P("exp", "rep", None),
        ),
        out_specs=(P("exp", "rep"), P("exp", "rep"), P("exp", None, "rep"), P("exp", "rep", None)),
        check_vma=False,
    )
```

profile of v0, /device:TPU:2, one launch (start us, length us, event | category | flops | bytes accessed | tf_op | source)
XLA Modules:
  0.0 255.9 jit_solution(6075189790972760029)
XLA Ops:
  7.2 0.0 copy-start
  7.2 0.9 copy.37
  8.1 0.1 reshape.220
  8.3 0.1 eq.70
  8.4 0.6 reduce-window.6
  9.0 0.2 slice_reduce_fusion
  9.2 0.1 convert_reduce_fusion
  9.4 0.7 copy.41
  10.1 7.5 %all-to-all-start = ((bf16[16,1,2]{2,1,0:T(2,128)(2,1)}), bf16[16,1,2]{2,1,0:T(2,128)(2,1)S(1)}, u32[]{:S(2)}, u32[]{:S(2)}) async-start(bf16[16,1,2]{2,1,0:T(2,128)(2,1)} %copy.41), calls=%async_computation | async-start | bytes 16384 | tf_op jit(solution)/shard_map/all_to_all | solution.py:79
  17.6 0.1 reduce_sum.53
  17.7 0.1 copy.40
  17.8 0.7 multiply_add_fusion.1
  18.5 0.1 fusion.23
  18.6 3.1 %convolution_convert_fusion.1 = bf16[512,2048]{1,0:T(8,128)(2,1)} fusion(bf16[512,128]{1,0:T(8,128)(2,1)S(1)} %fusion.23, bf16[128,2048]{1,0:T(8,128)(2,1)} %param.6), kind=kOutput, calls=%fused_computation.1 | convolution fusion | flops 269484032 | bytes 2752512 | tf_op jit(solution)/shard_map/dot_general | solution.py:65
  21.6 2.1 all-to-all-done
  23.7 0.0 copy-start.2
  23.7 0.0 copy-start.1
  23.7 5.7 %all-to-all-start.1 = ((bf16[16,32,2048]{2,1,0:T(8,128)(2,1)}), bf16[16,32,2048]{2,1,0:T(8,128)(2,1)}, u32[]{:S(2)}, u32[]{:S(2)}) async-start(bf16[16,32,2048]{2,1,0:T(8,128)(2,1)} %bitcast.82), calls=%async_computation.1 | async-start | bytes 4194304 | tf_op jit(solution)/shard_map/all_to_all | solution.py:69
  29.5 0.0 copy-done.2
  29.5 0.1 copy.43
  29.6 0.1 mul.74
  29.7 0.0 copy-done.1
  29.8 2.4 mul.76
  32.1 3.7 %mul.77 = f32[256,2048]{1,0:T(8,128)} reshape(f32[128,2,2048]{2,1,0:T(2,128)} %mul.76) | data formatting | bytes 4194304 | tf_op jit(solution)/shard_map/mul | solution.py:59
  35.8 3.7 %convolution_convert_fusion = bf16[512,2048]{1,0:T(8,128)(2,1)} fusion(f32[256,2048]{1,0:T(8,128)} %mul.77, f32[256]{0:T(256)S(1)} %mul.74, s32[256]{0:T(256)S(1)} %multiply_add_fusion), kind=kOutput, calls=%fused_computation | convolution fusion | flops 539099136 | bytes 4196352 | tf_op jit(solution)/shard_map/dot_general | solution.py:66
  39.5 16.2 %all-to-all-done.1 = bf16[16,32,2048]{2,1,0:T(8,128)(2,1)} async-done(((bf16[16,32,2048]{2,1,0:T(8,128)(2,1)}), bf16[16,32,2048]{2,1,0:T(8,128)(2,1)}, u32[]{:S(2)}, u32[]{:S(2)}) %all-to-all-start.1) | async-done | bytes 2097184 | tf_op jit(solution)/shard_map/all_to_all | solution.py:69
  55.7 7.8 %all-to-all-start.3 = ((bf16[16,32,2048]{2,1,0:T(8,128)(2,1)}), bf16[16,32,2048]{2,1,0:T(8,128)(2,1)}, u32[]{:S(2)}, u32[]{:S(2)}) async-start(bf16[16,32,2048]{2,1,0:T(8,128)(2,1)} %bitcast.81), calls=%async_computation.3 | async-start | bytes 4194304 | tf_op jit(solution)/shard_map/all_to_all | solution.py:72
  63.4 0.0 all-reduce.3.cloned.1.call-start
  63.5 0.1 copy.42
  63.6 0.1 iota_compare_fusion.6
  63.7 0.1 lt.37
  63.7 3.5 %fusion.6 = f32[512,512]{1,0:T(8,128)S(1)} fusion(bf16[512,2048]{1,0:T(8,128)(2,1)} %bitcast.8, bf16[1,2048,512]{2,1,0:T(8,128)(2,1)} %param.10), kind=kOutput, calls=%fused_computation.12 | convolution fusion | flops 1073741824 | bytes 5242880 | tf_op jit(solution)/shard_map/dot_general | solution.py:21
  67.2 0.0 copy-start.4
  67.2 1.0 copy-done.4
  68.2 0.0 copy-done
  68.2 2.6 %convolution_convert_fusion.5 = bf16[512,2048]{1,0:T(8,128)(2,1)} fusion(bf16[1,512,2048]{2,1,0:T(8,128)(2,1)S(1)} %copy-done, f32[512,512]{1,0:T(8,128)S(1)} %fusion.6, pred[512]{0:T(512)(128)(4,1)S(1)} %lt.37), kind=kOutput, calls=%fused_computation.5 | convolution fusion | flops 1076363264 | bytes 5243392 | tf_op jit(solution)/shard_map/dot_general | solution.py:25
  70.8 18.6 %all-to-all-done.3 = bf16[16,32,2048]{2,1,0:T(8,128)(2,1)} async-done(((bf16[16,32,2048]{2,1,0:T(8,128)(2,1)}), bf16[16,32,2048]{2,1,0:T(8,128)(2,1)}, u32[]{:S(2)}, u32[]{:S(2)}) %all-to-all-start.3) | async-done | bytes 2097184 | tf_op jit(solution)/shard_map/all_to_all | solution.py:72
  89.4 0.0 copy-start.3
  89.4 3.5 %fusion.14 = bf16[512,512]{1,0:T(8,128)(2,1)S(1)} fusion(bf16[512,2048]{1,0:T(8,128)(2,1)} %bitcast.15, bf16[1,512,2048]{2,1,0:T(8,128)(2,1)S(1)} %copy-done, f32[512,512]{1,0:T(8,128)} %copy-done.4, pred[512]{0:T(512)(128)(4,1)S(1)} %lt.37), kind=kOutput, calls=%fused_computation.17 | convolution fusion | flops 1076363264 | bytes 5767680 | tf_op jit(solution)/shard_map/dot_general | solution.py:26
  92.9 0.0 copy-done.3
  92.9 2.7 %convolution_convert_fusion.4 = bf16[512,2048]{1,0:T(8,128)(2,1)} fusion(bf16[512,512]{1,0:T(8,128)(2,1)S(1)} %fusion.14, bf16[1,2048,512]{2,1,0:T(8,128)(2,1)S(1)} %copy-done.3), kind=kOutput, calls=%fused_computation.4 | convolution fusion | flops 1074790400 | bytes 4718592 | tf_op jit(solution)/shard_map/dot_general | solution.py:40
  95.6 0.0 all-reduce.3.cloned.1.call-update
  95.6 4.7 %fusion.1 = bf16[1,512,2048]{2,1,0:T(8,128)(2,1)} fusion(bf16[512,2048]{1,0:T(8,128)(2,1)} %bitcast.15, f32[512,512]{1,0:T(8,128)} %copy-done.4, pred[512]{0:T(512)(128)(4,1)S(1)} %lt.37), kind=kOutput, calls=%fused_computation.7 | convolution fusion | flops 1076363264 | bytes 5243392 | tf_op jit(solution)/shard_map/dot_general | solution.py:31
  100.3 119.4 %all-reduce.3.cloned.1.call-done = (bf16[512,2048]{1,0:T(8,128)(2,1)}, bf16[512,2048]{1,0:T(8,128)(2,1)}) async-done(((bf16[512,2048]{1,0:T(8,128)(2,1)}, bf16[512,2048]{1,0:T(8,128)(2,1)}), (bf16[512,2048]{1,0:T(8,128)(2,1)}, bf16[512,2048]{1,0:T(8,128)(2,1)})) %all-reduce.3.cloned.1.call-update) | async-done | bytes 4194320 | tf_op jit(solution)/shard_map/psum | solution.py:92
  219.7 1.6 convert_convert_fusion.1
  221.2 7.3 %all-to-all-start.2 = ((bf16[16,32,128]{2,1,0:T(8,128)(2,1)}), bf16[16,32,128]{2,1,0:T(8,128)(2,1)S(1)}, u32[]{:S(2)}, u32[]{:S(2)}) async-start(bf16[16,32,128]{2,1,0:T(8,128)(2,1)} %bitcast.11), calls=%async_computation.2 | async-start | bytes 262144 | tf_op jit(solution)/shard_map/all_to_all | solution.py:99
  228.5 4.2 %fusion = bf16[1,2048,512]{2,1,0:T(8,128)(2,1)} fusion(bf16[512,2048]{1,0:T(8,128)(2,1)} %bitcast.8, bf16[512,512]{1,0:T(8,128)(2,1)S(1)} %fusion.14), kind=kOutput, calls=%fused_computation.6 | convolution fusion | flops 1074790400 | bytes 4718592 | tf_op jit(solution)/shard_map/dot_general | solution.py:34
  232.7 1.5 convert_convert_fusion
  234.3 0.9 all-to-all-done.2
  235.1 6.4 %all-to-all-start.4 = ((bf16[16,32,128]{2,1,0:T(8,128)(2,1)}), bf16[16,32,128]{2,1,0:T(8,128)(2,1)S(1)}, u32[]{:S(2)}, u32[]{:S(2)}) async-start(bf16[16,32,128]{2,1,0:T(8,128)(2,1)} %bitcast.16), calls=%async_computation.4 | async-start | bytes 262144 | tf_op jit(solution)/shard_map/all_to_all | solution.py:106
  241.5 0.9 fusion.17
  242.4 5.7 %all-to-all-done.4 = bf16[16,32,128]{2,1,0:T(8,128)(2,1)S(1)} async-done(((bf16[16,32,128]{2,1,0:T(8,128)(2,1)}), bf16[16,32,128]{2,1,0:T(8,128)(2,1)S(1)}, u32[]{:S(2)}, u32[]{:S(2)}) %all-to-all-start.4) | async-done | bytes 131104 | tf_op jit(solution)/shard_map/all_to_all | solution.py:106
  248.1 0.9 convolution_reduce_fusion
  (7 shorter events, 0.1 us)
Async XLA Ops:
  7.2 61.0 %copy-start = (bf16[1,512,2048]{2,1,0:T(8,128)(2,1)S(1)}, bf16[1,512,2048]{2,1,0:T(8,128)(2,1)}, u32[]{:S(2)}) copy-start(bf16[1,512,2048]{2,1,0:T(8,128)(2,1)} %param.11) | copy-start | bytes 6291460
  10.1 13.6 %all-to-all-start = ((bf16[16,1,2]{2,1,0:T(2,128)(2,1)}), bf16[16,1,2]{2,1,0:T(2,128)(2,1)S(1)}, u32[]{:S(2)}, u32[]{:S(2)}) async-start(bf16[16,1,2]{2,1,0:T(2,128)(2,1)} %copy.41), calls=%async_computation | async-start | bytes 16384 | tf_op jit(solution)/shard_map/all_to_all | solution.py:79
  23.7 5.8 %copy-start.2 = (f32[128,2]{0,1:T(2,128)S(1)}, f32[128,2]{0,1:T(2,128)}, u32[]{:S(2)}) copy-start(f32[128,2]{0,1:T(2,128)} %param.8) | copy-start | bytes 3076
  23.7 6.0 %copy-start.1 = (bf16[128,2048]{1,0:T(8,128)(2,1)S(1)}, bf16[128,2048]{1,0:T(8,128)(2,1)}, u32[]{:S(2)}) copy-start(bf16[128,2048]{1,0:T(8,128)(2,1)} %param.9) | copy-start | bytes 1572868
  23.7 31.9 %all-to-all-start.1 = ((bf16[16,32,2048]{2,1,0:T(8,128)(2,1)}), bf16[16,32,2048]{2,1,0:T(8,128)(2,1)}, u32[]{:S(2)}, u32[]{:S(2)}) async-start(bf16[16,32,2048]{2,1,0:T(8,128)(2,1)} %bitcast.82), calls=%async_computation.1 | async-start | bytes 4194304 | tf_op jit(solution)/shard_map/all_to_all | solution.py:69
  55.7 33.7 %all-to-all-start.3 = ((bf16[16,32,2048]{2,1,0:T(8,128)(2,1)}), bf16[16,32,2048]{2,1,0:T(8,128)(2,1)}, u32[]{:S(2)}, u32[]{:S(2)}) async-start(bf16[16,32,2048]{2,1,0:T(8,128)(2,1)} %bitcast.81), calls=%async_computation.3 | async-start | bytes 4194304 | tf_op jit(solution)/shard_map/all_to_all | solution.py:72
  63.4 156.3 %all-reduce.3.cloned.1.call-start = ((), (), s32[]{:S(2)}) async-start(), calls=%async_computation.5 | async-start | bytes 8388608 | tf_op jit(solution)/shard_map/psum | solution.py:92
  67.2 1.0 copy-start.4
  89.4 3.5 %copy-start.3 = (bf16[1,2048,512]{2,1,0:T(8,128)(2,1)S(1)}, bf16[1,2048,512]{2,1,0:T(8,128)(2,1)}, u32[]{:S(2)}) copy-start(bf16[1,2048,512]{2,1,0:T(8,128)(2,1)} %param.10) | copy-start | bytes 6291460
  221.2 13.9 %all-to-all-start.2 = ((bf16[16,32,128]{2,1,0:T(8,128)(2,1)}), bf16[16,32,128]{2,1,0:T(8,128)(2,1)S(1)}, u32[]{:S(2)}, u32[]{:S(2)}) async-start(bf16[16,32,128]{2,1,0:T(8,128)(2,1)} %bitcast.11), calls=%async_computation.2 | async-start | bytes 262144 | tf_op jit(solution)/shard_map/all_to_all | solution.py:99
  235.1 13.0 %all-to-all-start.4 = ((bf16[16,32,128]{2,1,0:T(8,128)(2,1)}), bf16[16,32,128]{2,1,0:T(8,128)(2,1)S(1)}, u32[]{:S(2)}, u32[]{:S(2)}) async-start(bf16[16,32,128]{2,1,0:T(8,128)(2,1)} %bitcast.16), calls=%async_computation.4 | async-start | bytes 262144 | tf_op jit(solution)/shard_map/all_to_all | solution.py:106
Sparse Core Ops, SparseCore 0:
  95.7 123.8 all-reduce.2
where the time goes:
time: 257 us; the launch traced here: 256 us
  waiting for transfers between devices  163 us (63%)
  starting transfers between devices  34.7 us (14%)
  matrix products  29.7 us (12%)
  between operations  14.1 us (5%)
  local copies, waits for them, and re-layouts  9.78 us (4%)
  other arithmetic  4.77 us (2%)
    psum x1, waiting for transfers between devices, local(): lax.psum(out_part.astype(jnp.bfloat16), 'rep').astype(jnp.float32)  119 us
    all_to_all x1, waiting for transfers between devices, local(): lax.all_to_all(sent_grad.reshape(n_exp, capacity, width), 'exp', split_ax...  18.6 us
    all_to_all x1, waiting for transfers between devices, local(): lax.all_to_all(sent_in.reshape(n_exp, capacity, width), 'exp', split_axis...  16.2 us
    all_to_all x1, starting transfers between devices, local(): lax.all_to_all(sent_grad.reshape(n_exp, capacity, width), 'exp', split_ax...  7.76 us
    all_to_all x1, starting transfers between devices, local(): lax.all_to_all(count_parts, 'exp', split_axis=0, concat_axis=0, tiled=True)  7.48 us
    all_to_all x1, starting transfers between devices, local(): lax.all_to_all(summed_out.astype(jnp.bfloat16).reshape(n_exp, capacity, c...  7.27 us
    all_to_all x1, starting transfers between devices, local(): lax.all_to_all(summed_dx.astype(jnp.bfloat16).reshape(n_exp, capacity, co...  6.37 us
    mul x3, local copies, waits for them, and re-layouts, local(): gate_values[:, :, None] * grad_out[:, None, :].astype(jnp.float32)  6.2 us
  transfers between devices with their start and end apart: 6, of which 6 were waited for; matrix products, arithmetic and copies ran while one was open for 12% of the time, Pallas kernels for 0%

commit v1 on v0

--- a/solution.py
+++ b/solution.py
@@ -88,29 +88,18 @@
     out_part, dx_part, grad_up_e, grad_down_e = expert_math(
         rows_in, rows_grad, live_mask, up_weight, down_weight
     )
-    total_out, total_dx = (
-        lax.psum(out_part.astype(jnp.bfloat16), "rep").astype(jnp.float32),
-        lax.psum(dx_part.astype(jnp.bfloat16), "rep").astype(jnp.float32),
+    summed_out = lax.psum_scatter(
+        out_part.astype(jnp.bfloat16), "rep", scatter_dimension=1, tiled=True
     )
-    col_start = lax.axis_index("rep") * cols
-    summed_out = lax.dynamic_slice_in_dim(total_out, col_start, cols, 1)
-    summed_dx = lax.dynamic_slice_in_dim(total_dx, col_start, cols, 1)
-    back_out, back_dx = (
-        lax.all_to_all(
-            summed_out.astype(jnp.bfloat16).reshape(n_exp, capacity, cols),
-            "exp",
-            split_axis=0,
-            concat_axis=0,
-            tiled=True,
-        ),
-        lax.all_to_all(
-            summed_dx.astype(jnp.bfloat16).reshape(n_exp, capacity, cols),
-            "exp",
-            split_axis=0,
-            concat_axis=0,
-            tiled=True,
-        ),
+    summed_dx = lax.psum_scatter(
+        dx_part.astype(jnp.bfloat16), "rep", scatter_dimension=1, tiled=True
     )
+    both = jnp.concatenate([summed_out, summed_dx], axis=1)
+    back_both = lax.all_to_all(
+        both.reshape(n_exp, capacity, 2 * cols), "exp", split_axis=0, concat_axis=0, tiled=True
+    ).reshape(n_exp * capacity, 2 * cols)
+    back_out = back_both[:, :cols]
+    back_dx = back_both[:, cols:]
     pair_out = jnp.einsum(
         "st,sd->td",
         placed,

time: 257 us -> 217 us (0.84)
  waiting for transfers between devices: 163 us -> 97.3 us
  blocking collectives: 0 us -> 33.5 us
  starting transfers between devices: 34.7 us -> 20.6 us
  local copies, waits for them, and re-layouts: 9.78 us -> 21.8 us
  matrix products: 29.7 us -> 25.1 us
    psum x1 -> x0, waiting for transfers between devices: 119 us -> none  [local(): lax.psum(out_part.astype(jnp.bfloat16), 'rep').astype(jnp.float32)]
    unnamed x1 -> x4, waiting for transfers between devices: 0.02 us -> 66.3 us
    all_to_all x0 -> x1, blocking collectives: none -> 33.5 us  [local(): lax.all_to_all(sent_grad.reshape(n_exp, capacity, width), 'exp', split_ax...]
    all_to_all x3 -> x1, waiting for transfers between devices: 25.2 us -> 3.13 us  [local(): lax.all_to_all(both.reshape(n_exp, capacity, 2 * cols), 'exp', split_axis...]
    all_to_all x3 -> x1, starting transfers between devices: 21.4 us -> 7.48 us  [local(): lax.all_to_all(both.reshape(n_exp, capacity, 2 * cols), 'exp', split_axis...]
    unnamed x12 -> x20, local copies, waits for them, and re-layouts: 2.04 us -> 14.1 us
    all_to_all x1, waiting for transfers between devices: 16.2 us -> 25.9 us  [local(): lax.all_to_all(sent_in.reshape(n_exp, capacity, width), 'exp', split_axis...]
    convert_element_type x2 -> x0, other arithmetic: 3.1 us -> none  [the longest x1 1.55 us: local(): summed_out.astype(jnp.bfloat16).reshape(n_exp, capacity, cols)]
  transfers between devices with their start and end apart: 6 -> 5, of which waited for: 6 -> 5; matrix products, arithmetic and copies ran while one was open for 12% -> 14% of each run, Pallas kernels for 0% -> 0%
where the time goes in v1:
time: 217 us
  waiting for transfers between devices  97.3 us (45%)
  blocking collectives  33.5 us (15%)
  matrix products  25.1 us (12%)
  local copies, waits for them, and re-layouts  21.8 us (10%)
  starting transfers between devices  20.6 us (9%)
  between operations  14.2 us (7%)
  other arithmetic  4.07 us (2%)
    unnamed x4, waiting for transfers between devices  66.3 us
    all_to_all x1, blocking collectives, local(): lax.all_to_all(sent_grad.reshape(n_exp, capacity, width), 'exp', split_ax...  33.5 us
    all_to_all x1, waiting for transfers between devices, local(): lax.all_to_all(sent_in.reshape(n_exp, capacity, width), 'exp', split_axis...  25.9 us
    unnamed x20, local copies, waits for them, and re-layouts  14.1 us
    all_to_all x1, starting transfers between devices, local(): lax.all_to_all(count_parts, 'exp', split_axis=0, concat_axis=0, tiled=True)  7.48 us
    all_to_all x1, starting transfers between devices, local(): lax.all_to_all(both.reshape(n_exp, capacity, 2 * cols), 'exp', split_axis...  7.48 us
    mul x3, local copies, waits for them, and re-layouts, local(): gate_values[:, :, None] * grad_out[:, None, :].astype(jnp.float32)  6.16 us
    all_to_all x1, starting transfers between devices, local(): lax.all_to_all(sent_in.reshape(n_exp, capacity, width), 'exp', split_axis...  5.61 us
  transfers between devices with their start and end apart: 5, of which 5 were waited for; matrix products, arithmetic and copies ran while one was open for 14% of the time, Pallas kernels for 0%

profile of v1, /device:TPU:2, one launch (start us, length us, event | category | flops | bytes accessed | tf_op | source)
XLA Modules:
  0.0 216.6 jit_solution(4632287968296737551)
XLA Ops:
  7.2 0.0 copy-start
  7.2 0.9 copy.39
  8.1 0.1 reshape.195
  8.3 0.1 eq.48
  8.4 0.6 reduce-window.6
  9.0 0.2 slice_reduce_fusion
  9.2 0.1 convert_reduce_fusion
  9.4 0.7 copy.42
  10.1 7.5 %all-to-all-start = ((bf16[16,1,2]{2,1,0:T(2,128)(2,1)}), bf16[16,1,2]{2,1,0:T(2,128)(2,1)S(1)}, u32[]{:S(2)}, u32[]{:S(2)}) async-start(bf16[16,1,2]{2,1,0:T(2,128)(2,1)} %copy.42), calls=%async_computation | async-start | bytes 16384 | tf_op jit(solution)/shard_map/all_to_all | solution.py:79
  17.6 0.1 reduce_sum.55
  17.7 0.1 copy.44
  17.8 0.7 multiply_add_fusion
  18.5 0.1 fusion.21
  18.6 3.1 %convolution_convert_fusion.1 = bf16[512,2048]{1,0:T(8,128)(2,1)} fusion(bf16[512,128]{1,0:T(8,128)(2,1)S(1)} %fusion.21, bf16[128,2048]{1,0:T(8,128)(2,1)} %param.6), kind=kOutput, calls=%fused_computation.1 | convolution fusion | flops 269484032 | bytes 2752512 | tf_op jit(solution)/shard_map/dot_general | solution.py:65
  21.6 2.1 all-to-all-done
  23.7 5.6 %all-to-all-start.1 = ((bf16[16,32,2048]{2,1,0:T(8,128)(2,1)}), bf16[16,32,2048]{2,1,0:T(8,128)(2,1)}, u32[]{:S(2)}, u32[]{:S(2)}) async-start(bf16[16,32,2048]{2,1,0:T(8,128)(2,1)} %bitcast.76), calls=%async_computation.1 | async-start | bytes 4194304 | tf_op jit(solution)/shard_map/all_to_all | solution.py:69
  29.3 0.0 reduce-scatter.7.cloned.1.call-start
  29.4 0.1 copy.43
  29.5 0.1 iota_compare_fusion.7
  29.6 0.1 lt.33
  29.7 25.9 %all-to-all-done.1 = bf16[16,32,2048]{2,1,0:T(8,128)(2,1)} async-done(((bf16[16,32,2048]{2,1,0:T(8,128)(2,1)}), bf16[16,32,2048]{2,1,0:T(8,128)(2,1)}, u32[]{:S(2)}, u32[]{:S(2)}) %all-to-all-start.1) | async-done | bytes 2097184 | tf_op jit(solution)/shard_map/all_to_all | solution.py:69
  55.5 3.5 %fusion.6 = f32[512,512]{1,0:T(8,128)S(1)} fusion(bf16[512,2048]{1,0:T(8,128)(2,1)} %bitcast.7, bf16[1,2048,512]{2,1,0:T(8,128)(2,1)} %param.10), kind=kOutput, calls=%fused_computation.12 | convolution fusion | flops 1073741824 | bytes 5242880 | tf_op jit(solution)/shard_map/dot_general | solution.py:21
  59.0 0.0 copy-start.5
  59.0 1.0 copy-done.5
  60.0 0.0 copy-done
  60.0 2.6 %convolution_convert_fusion.5 = bf16[512,2048]{1,0:T(8,128)(2,1)} fusion(bf16[1,512,2048]{2,1,0:T(8,128)(2,1)S(1)} %copy-done, f32[512,512]{1,0:T(8,128)S(1)} %fusion.6, pred[512]{0:T(512)(128)(4,1)S(1)} %lt.33), kind=kOutput, calls=%fused_computation.5 | convolution fusion | flops 1076363264 | bytes 5243392 | tf_op jit(solution)/shard_map/dot_general | solution.py:25
  62.6 3.9 %copy.46 = bf16[512,2048]{0,1:T(8,128)(2,1)} copy(bf16[512,2048]{1,0:T(8,128)(2,1)} %convolution_convert_fusion.5) | data formatting | bytes 4194304
  66.6 0.0 copy-start.3
  66.6 0.0 copy-start.2
  66.6 0.0 reduce-scatter.7.cloned.1.call-update
  66.6 0.0 reduce-scatter.9.cloned.1.call-start
  66.6 0.6 copy-done.3
  67.2 0.1 copy.38
  67.4 0.1 mul.68
  67.5 0.1 copy-done.2
  67.6 2.4 %mul.70 = f32[128,2,2048]{2,1,0:T(2,128)} broadcast(bf16[128,2048]{1,0:T(8,128)(2,1)S(1)} %copy-done.2), dimensions={0,2} | broadcast | bytes 2621440 | tf_op jit(solution)/shard_map/mul | solution.py:59
  70.0 3.6 %mul.71 = f32[256,2048]{1,0:T(8,128)} reshape(f32[128,2,2048]{2,1,0:T(2,128)} %mul.70) | data formatting | bytes 4194304 | tf_op jit(solution)/shard_map/mul | solution.py:59
  73.6 2.4 %convolution_convert_fusion = bf16[512,2048]{1,0:T(8,128)(2,1)S(1)} fusion(f32[256,2048]{1,0:T(8,128)} %mul.71, f32[256]{0:T(256)S(1)} %mul.68, s32[256]{0:T(256)S(1)} %multiply_add_fusion.1), kind=kOutput, calls=%fused_computation | convolution fusion | flops 539099136 | bytes 4196352 | tf_op jit(solution)/shard_map/dot_general | solution.py:66
  76.0 0.0 copy-start.6
  76.0 33.5 %all_to_all.24 = bf16[16,32,2048]{2,1,0:T(8,128)(2,1)S(1)} all-to-all(bf16[16,32,2048]{2,1,0:T(8,128)(2,1)S(1)} %bitcast.78), channel_id=1, replica_groups=mesh['rep'=16,'exp'=16] {'exp'}, dimensions={0} | all-to-all | bytes 4194304 | tf_op jit(solution)/shard_map/all_to_all | solution.py:72
  109.5 0.0 copy-start.1
  109.5 1.3 copy-done.1
  110.8 0.0 copy-done.6
  110.8 0.0 copy-start.4
  110.8 1.5 fusion.14
  112.3 0.1 copy-done.4
  112.5 2.6 %convolution_convert_fusion.4 = bf16[512,2048]{1,0:T(8,128)(2,1)} fusion(bf16[512,512]{1,0:T(8,128)(2,1)S(1)} %fusion.14, bf16[1,2048,512]{2,1,0:T(8,128)(2,1)S(1)} %copy-done.4), kind=kOutput, calls=%fused_computation.4 | convolution fusion | flops 1074790400 | bytes 4718592 | tf_op jit(solution)/shard_map/dot_general | solution.py:40
  115.1 3.9 %copy.48 = bf16[512,2048]{0,1:T(8,128)(2,1)} copy(bf16[512,2048]{1,0:T(8,128)(2,1)} %convolution_convert_fusion.4) | data formatting | bytes 4194304
  119.0 0.0 reduce-scatter.9.cloned.1.call-update
  119.0 4.7 %fusion.1 = bf16[1,512,2048]{2,1,0:T(8,128)(2,1)} fusion(bf16[512,2048]{1,0:T(8,128)(2,1)} %bitcast.80, f32[512,512]{1,0:T(8,128)} %copy-done.5, pred[512]{0:T(512)(128)(4,1)S(1)} %lt.33), kind=kOutput, calls=%fused_computation.7 | convolution fusion | flops 1076363264 | bytes 5243392 | tf_op jit(solution)/shard_map/dot_general | solution.py:31
  123.7 5.7 %reduce-scatter.7.cloned.1.call-done = bf16[128,512]{1,0:T(8,128)(2,1)} async-done(((bf16[2048,512]{1,0:T(8,128)(2,1)}), bf16[128,512]{1,0:T(8,128)(2,1)}) %reduce-scatter.7.cloned.1.call-update) | async-done | bytes 131088
  129.3 1.0 copy.47
  130.4 60.5 %reduce-scatter.9.cloned.1.call-done = bf16[128,512]{1,0:T(8,128)(2,1)} async-done(((bf16[2048,512]{1,0:T(8,128)(2,1)}), bf16[128,512]{1,0:T(8,128)(2,1)}) %reduce-scatter.9.cloned.1.call-update) | async-done | bytes 131088
  190.9 1.0 copy.49
  191.9 0.8 pad_maximum_fusion
  192.7 7.5 %all-to-all-start.3 = ((bf16[16,32,256]{2,1,0:T(8,128)(2,1)}), bf16[16,32,256]{2,1,0:T(8,128)(2,1)S(1)}, u32[]{:S(2)}, u32[]{:S(2)}) async-start(bf16[16,32,256]{2,1,0:T(8,128)(2,1)} %bitcast.12), calls=%async_computation.3 | async-start | bytes 524288 | tf_op jit(solution)/shard_map/all_to_all | solution.py:98
  200.2 4.2 %fusion = bf16[1,2048,512]{2,1,0:T(8,128)(2,1)} fusion(bf16[512,2048]{1,0:T(8,128)(2,1)} %bitcast.7, bf16[512,512]{1,0:T(8,128)(2,1)S(1)} %fusion.14), kind=kOutput, calls=%fused_computation.6 | convolution fusion | flops 1074790400 | bytes 4718592 | tf_op jit(solution)/shard_map/dot_general | solution.py:34
  204.4 3.1 %all-to-all-done.3 = bf16[16,32,256]{2,1,0:T(8,128)(2,1)S(1)} async-done(((bf16[16,32,256]{2,1,0:T(8,128)(2,1)}), bf16[16,32,256]{2,1,0:T(8,128)(2,1)S(1)}, u32[]{:S(2)}, u32[]{:S(2)}) %all-to-all-start.3) | async-done | bytes 262176 | tf_op jit(solution)/shard_map/all_to_all | solution.py:98
  207.5 0.3 fusion.18
  207.8 0.3 fusion.19
  208.2 0.9 multiply_reduce_fusion
  209.0 0.8 reduce_sum.58
  (7 shorter events, 0.1 us)
Async XLA Ops:
  7.2 52.8 %copy-start = (bf16[1,512,2048]{2,1,0:T(8,128)(2,1)S(1)}, bf16[1,512,2048]{2,1,0:T(8,128)(2,1)}, u32[]{:S(2)}) copy-start(bf16[1,512,2048]{2,1,0:T(8,128)(2,1)} %param.11) | copy-start | bytes 6291460
  10.1 13.6 %all-to-all-start = ((bf16[16,1,2]{2,1,0:T(2,128)(2,1)}), bf16[16,1,2]{2,1,0:T(2,128)(2,1)S(1)}, u32[]{:S(2)}, u32[]{:S(2)}) async-start(bf16[16,1,2]{2,1,0:T(2,128)(2,1)} %copy.42), calls=%async_computation | async-start | bytes 16384 | tf_op jit(solution)/shard_map/all_to_all | solution.py:79
  23.7 31.8 %all-to-all-start.1 = ((bf16[16,32,2048]{2,1,0:T(8,128)(2,1)}), bf16[16,32,2048]{2,1,0:T(8,128)(2,1)}, u32[]{:S(2)}, u32[]{:S(2)}) async-start(bf16[16,32,2048]{2,1,0:T(8,128)(2,1)} %bitcast.76), calls=%async_computation.1 | async-start | bytes 4194304 | tf_op jit(solution)/shard_map/all_to_all | solution.py:69
  29.3 100.0 %reduce-scatter.7.cloned.1.call-start = ((), (), s32[]{:S(2)}) async-start(), calls=%async_computation.6 | async-start | bytes 2228224
  59.0 1.0 copy-start.5
  66.6 0.7 copy-start.3
  66.6 1.1 copy-start.2
  66.6 124.3 %reduce-scatter.9.cloned.1.call-start = ((), (), s32[]{:S(2)}) async-start(), calls=%async_computation.7 | async-start | bytes 2228224
  76.0 34.8 %copy-start.6 = (f32[512,512]{1,0:T(8,128)S(1)}, f32[512,512]{1,0:T(8,128)}, u32[]{:S(2)}) copy-start(f32[512,512]{1,0:T(8,128)} %copy-done.5) | copy-start | bytes 3145732
  109.5 1.3 copy-start.1
  110.8 1.6 copy-start.4
  192.7 14.8 %all-to-all-start.3 = ((bf16[16,32,256]{2,1,0:T(8,128)(2,1)}), bf16[16,32,256]{2,1,0:T(8,128)(2,1)S(1)}, u32[]{:S(2)}, u32[]{:S(2)}) async-start(bf16[16,32,256]{2,1,0:T(8,128)(2,1)} %bitcast.12), calls=%async_computation.3 | async-start | bytes 524288 | tf_op jit(solution)/shard_map/all_to_all | solution.py:98
Sparse Core Ops, SparseCore 0:
  66.7 62.5 reduce-scatter.6
  132.4 58.4 reduce-scatter.8
